TPU v7x, 512 devices: a whole 4x4x16 slice. The times are simulated.
512 devices in a mesh: tile: 64 (over z, x), image: 2 (over y_hi), tensor: 4 (over y_lo, core).
Axes of the slice: x: 4, y: 4 (y_hi: 2, y_lo: 2; y = y_hi * 2 + y_lo), z: 16, core: 2. Of those that a mesh axis runs over, the one named last changes fastest.
Arguments:
- latent: bfloat16 [2, 256, 640, 128], P('image', 'tile', 'tensor'), may hold values from -8 to 8
- tile_slot: int32 [2, 64], replicated, may hold values from 0 to 63, each once within a row
- tile_count: int32 [2], replicated, may hold values from 16 to 64, as said below
- merge_num: int32 [1], replicated, may hold values from 3 to 13
- conv_ema: bfloat16 [3, 3, 4, 2, 80, 640], P(None, None, 'tensor', 'image'), may hold values from -0.078125 to 0.078125
- conv_adjusted: bfloat16 [3, 3, 4, 2, 80, 640], P(None, None, 'tensor', 'image'), may hold values from -0.078125 to 0.078125
- query_ema: bfloat16 [640, 512], P('image', 'tensor'), may hold values from -4 to 4
- query_adjusted: bfloat16 [640, 512], P('image', 'tensor'), may hold values from -4 to 4
- kv_ema: bfloat16 [640, 2, 512], P('image', None, 'tensor'), may hold values from -4 to 4
- kv_adjusted: bfloat16 [640, 2, 512], P('image', None, 'tensor'), may hold values from -4 to 4
- out_ema: bfloat16 [640, 512], P('tensor', 'image'), may hold values from -0.25 to 0.25
- out_adjusted: bfloat16 [640, 512], P('tensor', 'image'), may hold values from -0.25 to 0.25
- norm_gain: bfloat16 [640], replicated, may hold values from 0.099609375 to 1.8984375
Outputs:
- denoised: bfloat16 [2, 256, 640, 128], P('image', 'tile', 'tensor')
Inputs may be any that keep to these rules, and one draw needn't show every extreme that they name: `tile_count`: the number of live tiles of each image; exactly one image has all 64 live, the others fewer. `tile_slot`: each row is a permutation of the tiles' vertical positions.
All inputs are finite; a program needn't handle non-finite values.
Results may differ from a plain program's by a relative error of at most 0.007.
The roundings to bfloat16 on the way count: a program that leaves them out, or rounds other values in their place, can miss the bound.
Values may be sent and summed in bfloat16 or wider, within the bound.
No kernel may reach another device: no remote copies, remote signals or barrier semaphores. Data moves between devices by JAX's collectives and lax.ppermute only.
A program may use at most 64 MiB of HBM per device.

v0:
```python
import jax
import jax.numpy as jnp
from jax import lax
from jax.sharding import PartitionSpec as P

HD = 64
POOL = 4


def blend(ema_part, adjusted_part, blend_ratio):
    base = ema_part.astype(jnp.float32)
    return (base + blend_ratio * (adjusted_part.astype(jnp.float32) - base)).astype(jnp.bfloat16)


def convolve(field, kernel, row_padding):
    return lax.conv_general_dilated(
        field[None],
        kernel,
        (1, 1),
        (row_padding, (1, 1)),
        dimension_numbers=("NHCW", "HWOI", "NHCW"),
        preferred_element_type=jnp.float32,
    )[0]


def slot_lookup(tile_ids, slot_row):
    tile_total = slot_row.shape[0]
    matches = tile_ids[:, None] == jnp.arange(tile_total, dtype=jnp.int32)[None, :]
    return jnp.sum(jnp.where(matches, slot_row[None, :], 0), axis=1)


def on_device(
    latent,
    tile_slot,
    tile_count,
    merge_num,
    conv_ema,
    conv_adjusted,
    query_ema,
    query_adjusted,
    kv_ema,
    kv_adjusted,
    out_ema,
    out_adjusted,
    norm_gain,
):
    image_index = lax.axis_index("image")
    tile_index = lax.axis_index("tile")
    slot_row = lax.dynamic_index_in_dim(tile_slot, image_index, 0, keepdims=False)
    live_count = lax.dynamic_index_in_dim(tile_count, image_index, 0, keepdims=False)
    my_slot = lax.dynamic_index_in_dim(slot_row, tile_index, 0, keepdims=False)
    live_flag = (my_slot < live_count).astype(jnp.float32)
    blend_ratio = merge_num[0].astype(jnp.float32) / 16.0
    gathered = (
        lax.all_gather(conv_ema, "image", axis=3, tiled=True),
        lax.all_gather(conv_adjusted, "image", axis=3, tiled=True),
        lax.all_gather(query_ema, "image", axis=0, tiled=True),
        lax.all_gather(query_adjusted, "image", axis=0, tiled=True),
        lax.all_gather(kv_ema, "image", axis=0, tiled=True),
        lax.all_gather(kv_adjusted, "image", axis=0, tiled=True),
        lax.all_gather(out_ema, "image", axis=1, tiled=True),
        lax.all_gather(out_adjusted, "image", axis=1, tiled=True),
    )
    conv_w = blend(gathered[0], gathered[1], blend_ratio)
    query_w = blend(gathered[2], gathered[3], blend_ratio)
    kv_w = blend(gathered[4], gathered[5], blend_ratio)
    out_w = blend(gathered[6], gathered[7], blend_ratio)
    conv_w = conv_w.reshape(3, 3, -1, conv_w.shape[-1])
    feats = latent[0]
    tile_rows, chan_shard, tile_cols = feats.shape
    activated = jax.nn.silu(feats.astype(jnp.float32)).astype(jnp.bfloat16)
    block_full = lax.all_gather(activated, "tensor", axis=1, tiled=True)
    rim_rows = jnp.stack([activated[0], activated[-1]])[None]
    shard_piece = lax.all_gather(rim_rows, "tile", axis=0, tiled=True)
    source = jnp.arange(shard_piece.shape[0], dtype=jnp.int32)
    source_slot = slot_lookup(source, slot_row)
    upper_w = (source_slot == my_slot - 1).astype(jnp.float32)
    lower_w = jnp.logical_and(source_slot == my_slot + 1, source_slot < live_count).astype(
        jnp.float32
    )
    piece_f = shard_piece.astype(jnp.float32)
    upper = jnp.einsum("n,ncw->cw", upper_w, piece_f[:, 1])
    lower = jnp.einsum("n,ncw->cw", lower_w, piece_f[:, 0])
    halo_rows = jnp.stack([upper, lower]).astype(jnp.bfloat16)
    halo_full = lax.all_gather(halo_rows, "tensor", axis=1, tiled=True)
    padded = jnp.concatenate([halo_full[0:1], block_full, halo_full[1:2]], axis=0)
    conv_out = convolve(padded, conv_w, (0, 0))
    section = (feats.astype(jnp.float32) + conv_out).astype(jnp.bfloat16)
    section_full = lax.all_gather(section, "tensor", axis=1, tiled=True)
    channels = section_full.shape[1]
    cells = tile_rows * tile_cols
    section_f = section_full.astype(jnp.float32)
    rows_f = jnp.transpose(section_f, (0, 2, 1)).reshape(cells, channels)
    root_mean = jnp.sqrt(jnp.mean(rows_f * rows_f, axis=-1) + 1e-06)
    normed = (rows_f * norm_gain.astype(jnp.float32) / root_mean[:, None]).astype(jnp.bfloat16)
    queries = (jnp.dot(normed, query_w, preferred_element_type=jnp.float32) * HD ** (-0.5)).astype(
        jnp.bfloat16
    )
    att_shard = queries.shape[1]
    head_count = att_shard // HD
    pooled = section_f.reshape(tile_rows // POOL, POOL, channels, tile_cols // POOL, POOL).mean(
        axis=(1, 4)
    )
    tok_count = pooled.shape[0] * pooled.shape[2]
    pooled = jnp.transpose(pooled, (0, 2, 1)).astype(jnp.bfloat16).reshape(tok_count, channels)
    kv_flat = kv_w.reshape(channels, 2 * att_shard)
    block_rows = min(512, cells)
    blocks = cells // block_rows
    query_blocks = queries.reshape(blocks, block_rows, head_count, HD)
    start_state = (
        jnp.full((blocks, block_rows, head_count), -1e30, jnp.float32),
        jnp.zeros((blocks, block_rows, head_count), jnp.float32),
        jnp.zeros((blocks, block_rows, head_count, HD), jnp.float32),
    )
    kv_rows = jnp.dot(
        lax.all_gather(pooled, "tile", axis=0, tiled=True),
        kv_flat,
        preferred_element_type=jnp.float32,
    ).astype(jnp.bfloat16)
    key_rows = kv_rows[:, :att_shard]
    key_total = key_rows.shape[0]
    key_tile = jnp.arange(key_total, dtype=jnp.int32) // tok_count
    key_live = slot_lookup(key_tile, slot_row) < live_count
    key_livef = key_live.astype(jnp.float32)
    key_heads = key_rows.reshape(key_total, head_count, HD)
    value_heads = kv_rows[:, att_shard:].reshape(key_total, head_count, HD)

    def per_block(inputs):
        query_part, max_part, total_part, accum_part = inputs
        max_list, total_list, accum_list = ([], [], [])
        for head_index in range(head_count):
            scores = lax.dot_general(
                query_part[:, head_index],
                key_heads[:, head_index],
                (((1,), (1,)), ((), ())),
                preferred_element_type=jnp.float32,
            )
            scores = jnp.where(key_live[None, :], scores, -1e30)
            max_new = jnp.maximum(max_part[:, head_index], jnp.max(scores, axis=1))
            expd = jnp.exp(scores - max_new[:, None]) * key_livef[None, :]
            shrink = jnp.exp(max_part[:, head_index] - max_new)
            max_list.append(max_new)
            total_list.append(total_part[:, head_index] * shrink + jnp.sum(expd, axis=1))
            accum_list.append(
                accum_part[:, head_index] * shrink[:, None]
                + jnp.dot(
                    expd.astype(jnp.bfloat16),
                    value_heads[:, head_index],
                    preferred_element_type=jnp.float32,
                )
            )
        return (
            jnp.stack(max_list, axis=1),
            jnp.stack(total_list, axis=1),
            jnp.stack(accum_list, axis=1),
        )

    final_state = lax.map(per_block, (query_blocks, start_state[0], start_state[1], start_state[2]))
    attended = (
        (final_state[2] / final_state[1][..., None]).astype(jnp.bfloat16).reshape(cells, att_shard)
    )
    shard_piece = jax.tree.map(
        lambda part: lax.all_gather(part, "tensor", axis=1, tiled=True), attended
    )
    weight_cols = lax.slice_in_dim(out_w, 0, shard_piece.shape[1], axis=1)
    projected = jnp.zeros((chan_shard, cells), jnp.float32) + lax.dot_general(
        weight_cols, shard_piece, (((1,), (1,)), ((), ())), preferred_element_type=jnp.float32
    )
    projected = jnp.transpose(projected.reshape(chan_shard, tile_rows, tile_cols), (1, 0, 2))
    final = (section.astype(jnp.float32) + projected) * live_flag
    return final.astype(jnp.bfloat16).reshape(1, tile_rows, chan_shard, tile_cols)


def solution(mesh):
    placed = (
        P("image", "tile", "tensor", None),
        P(),
        P(),
        P(),
        P(None, None, "tensor", "image", None, None),
        P(None, None, "tensor", "image", None, None),
        P("image", "tensor"),
        P("image", "tensor"),
        P("image", None, "tensor"),
        P("image", None, "tensor"),
        P("tensor", "image"),
        P("tensor", "image"),
        P(),
    )
    return jax.shard_map(
        on_device,
        mesh=mesh,
        in_specs=placed,
        out_specs=P("image", "tile", "tensor", None),
        check_vma=False,
    )
```

profile of v0, /device:TPU:1, one launch (start us, length us, event | category | flops | bytes accessed | tf_op | source)
XLA Modules:
  0.0 443.0 jit_solution(12450239543727953347)
XLA Ops:
  13.0 13.6 %all_gather.44 = bf16[4,640,128]{2,0,1:T(4,128)(2,1)S(1)} all-gather(bf16[4,160,128]{2,0,1:T(4,128)(2,1)S(1)} %copy.107), channel_id=1, replica_groups=mesh['tile'=64,'image'=2,'tensor'=4] {'tensor'}, dimensions={1}, use_global_device_ids=true | all-gather | bytes 819200 | tf_op jit(solution)/shard_map/all_gather | solution.py:72
  26.6 30.2 %all-gather.7.cloned.1.call-done = bf16[3,3,1,2,80,640]{5,4,3,2,1,0:T(8,128)(2,1)} async-done(((bf16[3,3,1,1,80,640]{5,4,3,2,1,0:T(8,128)(2,1)}), bf16[3,3,1,2,80,640]{5,4,3,2,1,0:T(8,128)(2,1)}) %all-gather.7.cloned.1.call-update) | async-done | bytes 1843216 | tf_op jit(solution)/shard_map/all_gather | solution.py:55
  56.8 43.6 %all-gather.9.cloned.1.call-done = bf16[3,3,1,2,80,640]{5,4,3,2,1,0:T(8,128)(2,1)} async-done(((bf16[3,3,1,1,80,640]{5,4,3,2,1,0:T(8,128)(2,1)}), bf16[3,3,1,2,80,640]{5,4,3,2,1,0:T(8,128)(2,1)}) %all-gather.9.cloned.1.call-update) | async-done | bytes 1843216 | tf_op jit(solution)/shard_map/all_gather | solution.py:56
  100.4 4.0 fusion.1
  104.4 139.5 %all-gather.11.cloned.1.call-done = bf16[128,160,128]{2,1,0:T(8,128)(2,1)} async-done(((bf16[2,160,128]{2,1,0:T(8,128)(2,1)}), bf16[128,160,128]{2,1,0:T(8,128)(2,1)}) %all-gather.11.cloned.1.call-update) | async-done | bytes 5242896 | tf_op jit(solution)/shard_map/all_gather | solution.py:74
  243.9 2.9 slice_bitcast_fusion.1
  247.6 1.4 fusion.8
  249.1 15.5 %all_gather.43 = bf16[2,640,128]{2,1,0:T(8,128)(2,1)S(1)} all-gather(bf16[2,160,128]{2,1,0:T(8,128)(2,1)S(1)} %pad_maximum_fusion.2), channel_id=1, replica_groups=mesh['tile'=64,'image'=2,'tensor'=4] {'tensor'}, dimensions={1}, use_global_device_ids=true | all-gather | bytes 409600 | tf_op jit(solution)/shard_map/all_gather | solution.py:85
  265.1 1.1 maximum_bitcast_fusion
  266.3 1.2 copy.129
  268.4 1.2 copy-done
  269.6 1.8 convolution_select_fusion
  272.6 8.1 %all_gather.49 = bf16[4,640,128]{2,0,1:T(4,128)(2,1)S(1)} all-gather(bf16[4,160,128]{2,0,1:T(4,128)(2,1)S(1)} %copy.115), channel_id=1, replica_groups=mesh['tile'=64,'image'=2,'tensor'=4] {'tensor'}, dimensions={1}, use_global_device_ids=true | all-gather | bytes 819200 | tf_op jit(solution)/shard_map/all_gather | solution.py:89
  283.9 6.1 %all_gather.50 = bf16[640,128]{1,0:T(8,128)(2,1)S(1)} all-gather(bf16[320,128]{1,0:T(8,128)(2,1)S(1)} %copy-done.4), channel_id=1, replica_groups=mesh['tile'=64,'image'=2,'tensor'=4] {'image'}, dimensions={0}, use_global_device_ids=true | all-gather | bytes 245760 | tf_op jit(solution)/shard_map/all_gather | solution.py:57
  289.9 5.5 %all_gather.51 = bf16[640,128]{1,0:T(8,128)(2,1)S(1)} all-gather(bf16[320,128]{1,0:T(8,128)(2,1)S(1)} %copy-done.5), channel_id=1, replica_groups=mesh['tile'=64,'image'=2,'tensor'=4] {'image'}, dimensions={0}, use_global_device_ids=true | all-gather | bytes 245760 | tf_op jit(solution)/shard_map/all_gather | solution.py:58
  295.4 5.5 %all_gather.47 = bf16[160,512]{1,0:T(8,128)(2,1)S(1)} all-gather(bf16[160,256]{1,0:T(8,128)(2,1)S(1)} %copy-done.6), channel_id=1, replica_groups=mesh['tile'=64,'image'=2,'tensor'=4] {'image'}, dimensions={1}, use_global_device_ids=true | all-gather | bytes 245760 | tf_op jit(solution)/shard_map/all_gather | solution.py:61
  300.9 5.5 %all_gather.48 = bf16[160,512]{1,0:T(8,128)(2,1)S(1)} all-gather(bf16[160,256]{1,0:T(8,128)(2,1)S(1)} %copy-done.7), channel_id=1, replica_groups=mesh['tile'=64,'image'=2,'tensor'=4] {'image'}, dimensions={1}, use_global_device_ids=true | all-gather | bytes 245760 | tf_op jit(solution)/shard_map/all_gather | solution.py:62
  306.3 6.4 %all_gather.53 = bf16[640,2,128]{2,1,0:T(2,128)(2,1)S(1)} all-gather(bf16[320,2,128]{2,1,0:T(2,128)(2,1)S(1)} %copy-done.2), channel_id=1, replica_groups=mesh['tile'=64,'image'=2,'tensor'=4] {'image'}, dimensions={0}, use_global_device_ids=true | all-gather | bytes 491520 | tf_op jit(solution)/shard_map/all_gather | solution.py:59
  312.7 6.9 %all_gather.54 = bf16[640,2,128]{2,1,0:T(2,128)(2,1)S(1)} all-gather(bf16[320,2,128]{2,1,0:T(2,128)(2,1)S(1)} %copy-done.3), channel_id=1, replica_groups=mesh['tile'=64,'image'=2,'tensor'=4] {'image'}, dimensions={0}, use_global_device_ids=true | all-gather | bytes 491520 | tf_op jit(solution)/shard_map/all_gather | solution.py:60
  321.7 88.4 %all-gather.13.cloned.1.call-done = bf16[1,2048,640]{2,1,0:T(8,128)(2,1)} async-done(((bf16[1,32,640]{2,1,0:T(8,128)(2,1)}), bf16[1,2048,640]{2,1,0:T(8,128)(2,1)}) %all-gather.13.cloned.1.call-update) | async-done | bytes 2621456 | tf_op jit(solution)/shard_map/all_gather | solution.py:116
  410.2 2.8 fusion.12
  413.7 1.1 select_reduce_fusion.1
  414.8 2.1 fusion.2
  419.2 16.3 %all_gather.55 = bf16[512,512]{0,1:T(8,128)(2,1)S(1)} all-gather(bf16[512,128]{0,1:T(8,128)(2,1)S(1)} %fusion.63), channel_id=1, replica_groups=mesh['tile'=64,'image'=2,'tensor'=4] {'tensor'}, dimensions={1}, use_global_device_ids=true | all-gather | bytes 655360 | tf_op jit(solution)/shard_map/all_gather | solution.py:163
  (81 shorter events, 15.8 us)
Async XLA Ops:
  6.5 3.4 copy-start.9
  6.5 4.5 %copy-start.10 = (s32[2]{0:T(128)S(1)}, s32[2]{0:T(128)}, u32[]{:S(2)}) copy-start(s32[2]{0:T(128)} %param.15) | copy-start | bytes 28
  6.5 50.2 %all-gather.7.cloned.1.call-start = ((), (), s32[]{:S(2)}) async-start(), calls=%async_computation | async-start | bytes 2764800 | tf_op jit(solution)/shard_map/all_gather | solution.py:55
  7.3 93.1 %all-gather.9.cloned.1.call-start = ((), (), s32[]{:S(2)}) async-start(), calls=%async_computation.1 | async-start | bytes 2764800 | tf_op jit(solution)/shard_map/all_gather | solution.py:56
  8.0 235.9 %all-gather.11.cloned.1.call-start = ((), (), s32[]{:S(2)}) async-start(), calls=%async_computation.2 | async-start | bytes 5324800 | tf_op jit(solution)/shard_map/all_gather | solution.py:74
  9.8 400.4 %all-gather.13.cloned.1.call-start = ((), (), s32[]{:S(2)}) async-start(), calls=%async_computation.3 | async-start | bytes 2662400 | tf_op jit(solution)/shard_map/all_gather | solution.py:116
  267.7 0.7 copy-start.11
  268.1 1.5 copy-start
  271.5 0.9 copy-start.1
  272.4 11.4 %copy-start.8 = (bf16[640]{0:T(1024)(128)(2,1)S(1)}, bf16[640]{0:T(1024)(128)(2,1)}, u32[]{:S(2)}) copy-start(bf16[640]{0:T(1024)(128)(2,1)} %param.25) | copy-start | bytes 3844
  272.4 11.4 %copy-start.4 = (bf16[320,128]{1,0:T(8,128)(2,1)S(1)}, bf16[320,128]{1,0:T(8,128)(2,1)}, u32[]{:S(2)}) copy-start(bf16[320,128]{1,0:T(8,128)(2,1)} %param.19) | copy-start | bytes 245764
  272.5 17.5 %copy-start.5 = (bf16[320,128]{1,0:T(8,128)(2,1)S(1)}, bf16[320,128]{1,0:T(8,128)(2,1)}, u32[]{:S(2)}) copy-start(bf16[320,128]{1,0:T(8,128)(2,1)} %param.20) | copy-start | bytes 245764
  272.5 22.9 %copy-start.6 = (bf16[160,256]{1,0:T(8,128)(2,1)S(1)}, bf16[160,256]{1,0:T(8,128)(2,1)}, u32[]{:S(2)}) copy-start(bf16[160,256]{1,0:T(8,128)(2,1)} %param.23) | copy-start | bytes 245764
  272.6 28.3 %copy-start.7 = (bf16[160,256]{1,0:T(8,128)(2,1)S(1)}, bf16[160,256]{1,0:T(8,128)(2,1)}, u32[]{:S(2)}) copy-start(bf16[160,256]{1,0:T(8,128)(2,1)} %param.24) | copy-start | bytes 245764
  272.6 33.7 %copy-start.2 = (bf16[320,2,128]{2,1,0:T(2,128)(2,1)S(1)}, bf16[320,2,128]{2,1,0:T(2,128)(2,1)}, u32[]{:S(2)}) copy-start(bf16[320,2,128]{2,1,0:T(2,128)(2,1)} %param.21) | copy-start | bytes 491524
  280.7 32.0 %copy-start.3 = (bf16[320,2,128]{2,1,0:T(2,128)(2,1)S(1)}, bf16[320,2,128]{2,1,0:T(2,128)(2,1)}, u32[]{:S(2)}) copy-start(bf16[320,2,128]{2,1,0:T(2,128)(2,1)} %param.22) | copy-start | bytes 491524
Sparse Core Ops, SparseCore 0:
  9.4 47.2 all-gather.6
  58.9 41.4 all-gather.8
  103.3 140.5 all-gather.10
  282.8 127.3 all-gather.12
where the time goes:
time: 443 us
  waiting for transfers between devices  303 us (68%)
  blocking collectives  89.3 us (20%)
  between operations  16.5 us (4%)
  other arithmetic  12.5 us (3%)
  matrix products  11.4 us (3%)
  local copies, waits for them, and re-layouts  10.1 us (2%)
    all_gather x1, waiting for transfers between devices, on_device(): shard_piece = lax.all_gather(rim_rows, 'tile', axis=0, tiled=True)  140 us
    all_gather x1, waiting for transfers between devices, on_device(): lax.all_gather(pooled, 'tile', axis=0, tiled=True)  88.4 us
    all_gather x1, waiting for transfers between devices, on_device(): lax.all_gather(conv_adjusted, 'image', axis=3, tiled=True)  43.6 us
    all_gather x1, waiting for transfers between devices, on_device(): lax.all_gather(conv_ema, 'image', axis=3, tiled=True)  30.2 us
    all_gather x1, blocking collectives, on_device(): lax.all_gather(part, 'tensor', axis=1, tiled=True)  16.3 us
    all_gather x1, blocking collectives, on_device(): halo_full = lax.all_gather(halo_rows, 'tensor', axis=1, tiled=True)  15.5 us
    all_gather x1, blocking collectives, on_device(): block_full = lax.all_gather(activated, 'tensor', axis=1, tiled=True)  13.6 us
  transfers between devices with their start and end apart: 4, of which 4 were waited for; matrix products, arithmetic and copies ran while one was open for 2% of the time, Pallas kernels for 0%

commit v1 on v0

--- a/solution.py
+++ b/solution.py
@@ -53,7 +53,10 @@
     blend_ratio = merge_num[0].astype(jnp.float32) / 16.0
     gathered = (
         lax.all_gather(conv_ema, "image", axis=3, tiled=True),
-        lax.all_gather(conv_adjusted, "image", axis=3, tiled=True),
+        jnp.concatenate(
+            lax.all_to_all(jnp.stack([conv_adjusted] * lax.axis_size("image")), "image", 0, 0),
+            axis=3,
+        ),
         lax.all_gather(query_ema, "image", axis=0, tiled=True),
         lax.all_gather(query_adjusted, "image", axis=0, tiled=True),
         lax.all_gather(kv_ema, "image", axis=0, tiled=True),

time: 443 us -> 411 us (0.928)
  waiting for transfers between devices: 303 us -> 245 us
  blocking collectives: 89.3 us -> 107 us
  starting transfers between devices: 0.12 us -> 5.18 us
    all_gather x1 -> x0, waiting for transfers between devices: 43.6 us -> none  [on_device(): lax.all_gather(conv_adjusted, 'image', axis=3, tiled=True)]
    all_gather x1, blocking collectives: 13.6 us -> 31.2 us  [on_device(): block_full = lax.all_gather(activated, 'tensor', axis=1, tiled=True)]
    all_gather x1, waiting for transfers between devices: 30.2 us -> 13.1 us  [on_device(): lax.all_gather(conv_ema, 'image', axis=3, tiled=True)]
    all_to_all x0 -> x1, starting transfers between devices: none -> 5.14 us  [on_device(): lax.all_to_all(jnp.stack([conv_adjusted] * lax.axis_size('image')), 'imag...]
  transfers between devices with their start and end apart: 4 -> 4, of which waited for: 4 -> 3; matrix products, arithmetic and copies ran while one was open for 2% -> 3% of each run, Pallas kernels for 0% -> 0%
where the time goes in v1:
time: 411 us; the launch traced here: 410 us
  waiting for transfers between devices  245 us (60%)
  blocking collectives  107 us (26%)
  between operations  16.6 us (4%)
  other arithmetic  15 us (4%)
  matrix products  11.3 us (3%)
  local copies, waits for them, and re-layouts  10.1 us (2%)
  starting transfers between devices  5.18 us (1%)
    all_gather x1, waiting for transfers between devices, on_device(): shard_piece = lax.all_gather(rim_rows, 'tile', axis=0, tiled=True)  143 us
    all_gather x1, waiting for transfers between devices, on_device(): lax.all_gather(pooled, 'tile', axis=0, tiled=True)  88.5 us
    all_gather x1, blocking collectives, on_device(): block_full = lax.all_gather(activated, 'tensor', axis=1, tiled=True)  31.2 us
    all_gather x1, blocking collectives, on_device(): lax.all_gather(part, 'tensor', axis=1, tiled=True)  16.3 us
    all_gather x1, blocking collectives, on_device(): halo_full = lax.all_gather(halo_rows, 'tensor', axis=1, tiled=True)  15.5 us
    all_gather x1, waiting for transfers between devices, on_device(): lax.all_gather(conv_ema, 'image', axis=3, tiled=True)  13.1 us
  transfers between devices with their start and end apart: 4, of which 3 were waited for; matrix products, arithmetic and copies ran while one was open for 3% of the time, Pallas kernels for 0%

profile of v1, /device:TPU:1, one launch (start us, length us, event | category | flops | bytes accessed | tf_op | source)
XLA Modules:
  0.0 410.0 jit_solution(10972241609922226367)
XLA Ops:
  9.0 3.0 pad_maximum_fusion
  12.0 5.1 %all-to-all-start = ((bf16[2,3,3,1,1,80,640]{6,5,2,1,4,3,0:T(8,128)(2,1)}), bf16[2,3,3,1,1,80,640]{6,5,2,1,4,3,0:T(8,128)(2,1)S(1)}, u32[]{:S(2)}, u32[]{:S(2)}) async-start(bf16[2,3,3,1,1,80,640]{6,5,2,1,4,3,0:T(8,128)(2,1)} %pad_maximum_fusion), calls=%async_computation | async-start | bytes 3686400 | tf_op jit(solution)/shard_map/all_to_all | solution.py:57
  20.6 31.2 %all_gather.41 = bf16[4,640,128]{2,0,1:T(4,128)(2,1)S(1)} all-gather(bf16[4,160,128]{2,0,1:T(4,128)(2,1)S(1)} %copy.120), channel_id=1, replica_groups=mesh['tile'=64,'image'=2,'tensor'=4] {'tensor'}, dimensions={1}, use_global_device_ids=true | all-gather | bytes 819200 | tf_op jit(solution)/shard_map/all_gather | solution.py:75
  51.7 13.1 %all-gather.6.cloned.1.call-done = bf16[3,3,1,2,80,640]{5,4,3,1,0,2:T(8,128)(2,1)} async-done(((bf16[3,3,1,1,80,640]{5,4,3,1,0,2:T(8,128)(2,1)}), bf16[3,3,1,2,80,640]{5,4,3,1,0,2:T(8,128)(2,1)}) %all-gather.6.cloned.1.call-update) | async-done | bytes 1843216 | tf_op jit(solution)/shard_map/all_gather | solution.py:55
  64.8 3.5 fusion.1
  68.3 142.7 %all-gather.8.cloned.1.call-done = bf16[128,160,128]{2,1,0:T(8,128)(2,1)} async-done(((bf16[2,160,128]{2,1,0:T(8,128)(2,1)}), bf16[128,160,128]{2,1,0:T(8,128)(2,1)}) %all-gather.8.cloned.1.call-update) | async-done | bytes 5242896 | tf_op jit(solution)/shard_map/all_gather | solution.py:77
  211.0 2.9 slice_bitcast_fusion.1
  214.7 1.4 fusion.8
  216.1 15.5 %all_gather.40 = bf16[2,640,128]{2,1,0:T(8,128)(2,1)S(1)} all-gather(bf16[2,160,128]{2,1,0:T(8,128)(2,1)S(1)} %pad_maximum_fusion.3), channel_id=1, replica_groups=mesh['tile'=64,'image'=2,'tensor'=4] {'tensor'}, dimensions={1}, use_global_device_ids=true | all-gather | bytes 409600 | tf_op jit(solution)/shard_map/all_gather | solution.py:88
  232.2 1.1 maximum_bitcast_fusion
  233.3 1.2 copy.144
  235.5 1.2 copy-done
  236.7 1.8 convolution_select_fusion
  239.7 8.1 %all_gather.45 = bf16[4,640,128]{2,0,1:T(4,128)(2,1)S(1)} all-gather(bf16[4,160,128]{2,0,1:T(4,128)(2,1)S(1)} %copy.130), channel_id=1, replica_groups=mesh['tile'=64,'image'=2,'tensor'=4] {'tensor'}, dimensions={1}, use_global_device_ids=true | all-gather | bytes 819200 | tf_op jit(solution)/shard_map/all_gather | solution.py:92
  250.9 6.1 %all_gather.46 = bf16[640,128]{1,0:T(8,128)(2,1)S(1)} all-gather(bf16[320,128]{1,0:T(8,128)(2,1)S(1)} %copy-done.4), channel_id=1, replica_groups=mesh['tile'=64,'image'=2,'tensor'=4] {'image'}, dimensions={0}, use_global_device_ids=true | all-gather | bytes 245760 | tf_op jit(solution)/shard_map/all_gather | solution.py:60
  257.0 5.5 %all_gather.47 = bf16[640,128]{1,0:T(8,128)(2,1)S(1)} all-gather(bf16[320,128]{1,0:T(8,128)(2,1)S(1)} %copy-done.5), channel_id=1, replica_groups=mesh['tile'=64,'image'=2,'tensor'=4] {'image'}, dimensions={0}, use_global_device_ids=true | all-gather | bytes 245760 | tf_op jit(solution)/shard_map/all_gather | solution.py:61
  262.5 5.5 %all_gather.43 = bf16[160,512]{1,0:T(8,128)(2,1)S(1)} all-gather(bf16[160,256]{1,0:T(8,128)(2,1)S(1)} %copy-done.6), channel_id=1, replica_groups=mesh['tile'=64,'image'=2,'tensor'=4] {'image'}, dimensions={1}, use_global_device_ids=true | all-gather | bytes 245760 | tf_op jit(solution)/shard_map/all_gather | solution.py:64
  267.9 5.5 %all_gather.44 = bf16[160,512]{1,0:T(8,128)(2,1)S(1)} all-gather(bf16[160,256]{1,0:T(8,128)(2,1)S(1)} %copy-done.7), channel_id=1, replica_groups=mesh['tile'=64,'image'=2,'tensor'=4] {'image'}, dimensions={1}, use_global_device_ids=true | all-gather | bytes 245760 | tf_op jit(solution)/shard_map/all_gather | solution.py:65
  273.4 6.4 %all_gather.49 = bf16[640,2,128]{2,1,0:T(2,128)(2,1)S(1)} all-gather(bf16[320,2,128]{2,1,0:T(2,128)(2,1)S(1)} %copy-done.2), channel_id=1, replica_groups=mesh['tile'=64,'image'=2,'tensor'=4] {'image'}, dimensions={0}, use_global_device_ids=true | all-gather | bytes 491520 | tf_op jit(solution)/shard_map/all_gather | solution.py:62
  279.8 6.9 %all_gather.50 = bf16[640,2,128]{2,1,0:T(2,128)(2,1)S(1)} all-gather(bf16[320,2,128]{2,1,0:T(2,128)(2,1)S(1)} %copy-done.3), channel_id=1, replica_groups=mesh['tile'=64,'image'=2,'tensor'=4] {'image'}, dimensions={0}, use_global_device_ids=true | all-gather | bytes 491520 | tf_op jit(solution)/shard_map/all_gather | solution.py:63
  288.7 88.5 %all-gather.10.cloned.1.call-done = bf16[1,2048,640]{2,1,0:T(8,128)(2,1)} async-done(((bf16[1,32,640]{2,1,0:T(8,128)(2,1)}), bf16[1,2048,640]{2,1,0:T(8,128)(2,1)}) %all-gather.10.cloned.1.call-update) | async-done | bytes 2621456 | tf_op jit(solution)/shard_map/all_gather | solution.py:119
  377.2 2.8 fusion.12
  381.9 2.1 fusion.2
  386.2 16.3 %all_gather.51 = bf16[512,512]{0,1:T(8,128)(2,1)S(1)} all-gather(bf16[512,128]{0,1:T(8,128)(2,1)S(1)} %fusion.63), channel_id=1, replica_groups=mesh['tile'=64,'image'=2,'tensor'=4] {'tensor'}, dimensions={1}, use_global_device_ids=true | all-gather | bytes 655360 | tf_op jit(solution)/shard_map/all_gather | solution.py:166
  (81 shorter events, 16.1 us)
Async XLA Ops:
  6.5 58.3 %all-gather.6.cloned.1.call-start = ((), (), s32[]{:S(2)}) async-start(), calls=%async_computation.1 | async-start | bytes 2764800 | tf_op jit(solution)/shard_map/all_gather | solution.py:55
  7.3 203.8 %all-gather.8.cloned.1.call-start = ((), (), s32[]{:S(2)}) async-start(), calls=%async_computation.2 | async-start | bytes 5324800 | tf_op jit(solution)/shard_map/all_gather | solution.py:77
  12.0 5.3 %copy-start.9 = (s32[2,64]{1,0:T(2,128)S(1)}, s32[2,64]{1,0:T(2,128)}, u32[]{:S(2)}) copy-start(s32[2,64]{1,0:T(2,128)} %param.14) | copy-start | bytes 1540
  12.0 6.5 %copy-start.10 = (s32[2]{0:T(128)S(1)}, s32[2]{0:T(128)}, u32[]{:S(2)}) copy-start(s32[2]{0:T(128)} %param.15) | copy-start | bytes 28
  12.0 39.7 %all-to-all-start = ((bf16[2,3,3,1,1,80,640]{6,5,2,1,4,3,0:T(8,128)(2,1)}), bf16[2,3,3,1,1,80,640]{6,5,2,1,4,3,0:T(8,128)(2,1)S(1)}, u32[]{:S(2)}, u32[]{:S(2)}) async-start(bf16[2,3,3,1,1,80,640]{6,5,2,1,4,3,0:T(8,128)(2,1)} %pad_maximum_fusion), calls=%async_computation | async-start | bytes 3686400 | tf_op jit(solution)/shard_map/all_to_all | solution.py:57
  17.2 360.0 %all-gather.10.cloned.1.call-start = ((), (), s32[]{:S(2)}) async-start(), calls=%async_computation.3 | async-start | bytes 2662400 | tf_op jit(solution)/shard_map/all_gather | solution.py:119
  234.8 0.7 copy-start.11
  235.2 1.5 copy-start
  238.5 0.9 copy-start.1
  239.5 11.4 %copy-start.8 = (bf16[640]{0:T(1024)(128)(2,1)S(1)}, bf16[640]{0:T(1024)(128)(2,1)}, u32[]{:S(2)}) copy-start(bf16[640]{0:T(1024)(128)(2,1)} %param.25) | copy-start | bytes 3844
  239.5 11.4 %copy-start.4 = (bf16[320,128]{1,0:T(8,128)(2,1)S(1)}, bf16[320,128]{1,0:T(8,128)(2,1)}, u32[]{:S(2)}) copy-start(bf16[320,128]{1,0:T(8,128)(2,1)} %param.19) | copy-start | bytes 245764
  239.5 17.5 %copy-start.5 = (bf16[320,128]{1,0:T(8,128)(2,1)S(1)}, bf16[320,128]{1,0:T(8,128)(2,1)}, u32[]{:S(2)}) copy-start(bf16[320,128]{1,0:T(8,128)(2,1)} %param.20) | copy-start | bytes 245764
  239.5 22.9 %copy-start.6 = (bf16[160,256]{1,0:T(8,128)(2,1)S(1)}, bf16[160,256]{1,0:T(8,128)(2,1)}, u32[]{:S(2)}) copy-start(bf16[160,256]{1,0:T(8,128)(2,1)} %param.23) | copy-start | bytes 245764
  239.6 28.3 %copy-start.7 = (bf16[160,256]{1,0:T(8,128)(2,1)S(1)}, bf16[160,256]{1,0:T(8,128)(2,1)}, u32[]{:S(2)}) copy-start(bf16[160,256]{1,0:T(8,128)(2,1)} %param.24) | copy-start | bytes 245764
  239.6 33.8 %copy-start.2 = (bf16[320,2,128]{2,1,0:T(2,128)(2,1)S(1)}, bf16[320,2,128]{2,1,0:T(2,128)(2,1)}, u32[]{:S(2)}) copy-start(bf16[320,2,128]{2,1,0:T(2,128)(2,1)} %param.21) | copy-start | bytes 491524
  247.8 32.0 %copy-start.3 = (bf16[320,2,128]{2,1,0:T(2,128)(2,1)S(1)}, bf16[320,2,128]{2,1,0:T(2,128)(2,1)}, u32[]{:S(2)}) copy-start(bf16[320,2,128]{2,1,0:T(2,128)(2,1)} %param.22) | copy-start | bytes 491524
Sparse Core Ops, SparseCore 0:
  9.4 55.3 all-gather.5
  67.8 143.2 all-gather.7
  249.8 127.3 all-gather.9
